TPU v7x, 256 devices: a whole 4x4x8 slice. The times are simulated.
256 devices in a mesh: grp: 32 (over y, z_lo, core), tp: 8 (over x, z_hi).
Axes of the slice: x: 4, y: 4, z: 8 (z_hi: 2, z_lo: 4; z = z_hi * 4 + z_lo), core: 2. Of those that a mesh axis runs over, the one named last changes fastest.
Arguments:
- tok_ids: int32 [8192], P('grp'), may hold values from 0 to 16383
- accept: int32 [8192], P('grp'), may hold values 0 or 1
- sub_ids: int32 [8192], P('grp'), may hold values from 0 to 16383
- cache_len: int32 [32], replicated, may hold values from 256 to 3840, as said below
- spill: int32 [32], replicated, may hold values from 0 to 1792, as said below
- embed: bfloat16 [16384, 2048], P('grp', 'tp'), may hold values from -6 to 6
- attn_gain: float32 [2048], replicated, may hold values from 0.25 to 1.75
- w_query: bfloat16 [2048, 2048], P(None, 'tp'), may hold values from -0.125 to 0.125
- w_key: bfloat16 [2048, 512], P(None, 'tp'), as said below
- w_value: bfloat16 [2048, 512], P(None, 'tp'), as said below
- w_out: bfloat16 [2048, 2048], P('tp'), may hold values from -2.5 to 2.5
- mlp_gain: float32 [2048], replicated, may hold values from 0.25 to 1.75
- w_gate: bfloat16 [2048, 5632], P(None, 'tp'), may hold values from -0.125 to 0.125
- w_up: bfloat16 [2048, 5632], P(None, 'tp'), may hold values from -0.125 to 0.125
- w_down: bfloat16 [5632, 2048], P('tp'), may hold values from -0.078125 to 0.078125
- cache_keys: bfloat16 [65536, 512], P('grp', 'tp'), may hold values from -320 to 320, as said below
- cache_values: bfloat16 [65536, 512], P('grp', 'tp'), may hold values from -8 to 8, as said below
Outputs:
- first_out: bfloat16 [8192, 2048], P('grp', 'tp')
- second_out: bfloat16 [8192, 2048], P('grp', 'tp')
Inputs may be any that keep to these rules, and one draw needn't show every extreme that they name: Request g keeps cache_len[g] - spill[g] >= 256 positions in slots from 0 of store g and spill[g] positions in the last slots of store (g xor 1); for every g, cache_len[g] - spill[g] + spill[g xor 1] <= 2048. Of each pair of groups 2k, 2k + 1 at most one has spill above 0. `w_key`: the 2 stored copies of a key-value head are equal. `w_value`: the 2 stored copies of a key-value head are equal. `cache_keys`: the 2 stored copies of a key-value head are equal. `cache_values`: the 2 stored copies of a key-value head are equal.
All inputs are finite; a program needn't handle non-finite values. No bound on the sum of `accept` on one device may be relied on, other than what follows from the above.
Results may differ from a plain program's by a relative error of at most 0.024.
Values may be sent and summed in bfloat16 or wider, within the bound.
No kernel may reach another device: no remote copies, remote signals or barrier semaphores. Data moves between devices by JAX's collectives and lax.ppermute only.
A program may use at most 128 MiB of HBM per device.

v0:
```python
import jax
import jax.numpy as jnp
from jax import lax
from jax.sharding import PartitionSpec as P

HD = 64
EPSILON = 1e-05
SENTINEL = -1e30


def shifted(array, axis, step):
    n = lax.axis_size(axis)
    return lax.ppermute(array, axis, [(i, (i + step) % n) for i in range(n)])


def swapped(array, axis, bit):
    return lax.ppermute(array, axis, [(i, i ^ 1 << bit) for i in range(lax.axis_size(axis))])


def tp_gather(part):
    rows, width = part.shape
    n_x = lax.axis_size("tp") // 2
    me = lax.axis_index("tp")
    mine_x = me // 2
    partner = swapped(part, "tp", 0)
    low_first = me % 2 == 0
    pair = jnp.stack([jnp.where(low_first, part, partner), jnp.where(low_first, partner, part)])
    received = [pair] + [shifted(pair, "tp", 2 * k) for k in range(1, n_x)]
    stacked = jnp.stack(received)
    order = (mine_x - jnp.arange(n_x, dtype=jnp.int32)) % n_x
    full = jnp.take(stacked, order, axis=0)
    return full.transpose(2, 0, 1, 3).reshape(rows, n_x * 2 * width)


def tp_reduce(full):
    rows, total_width = full.shape
    n_x = lax.axis_size("tp") // 2
    me = lax.axis_index("tp")
    mine_x = me // 2
    pieces = full.reshape(rows, n_x, total_width // n_x)
    acc = jnp.take(pieces, mine_x, axis=1).astype(jnp.float32)
    for k in range(1, n_x):
        piece = jnp.take(pieces, (mine_x + k) % n_x, axis=1)
        acc = acc + shifted(piece, "tp", 2 * k).astype(jnp.float32)
    halves = acc.reshape(rows, 2, total_width // n_x // 2)
    low = me % 2 == 0
    mine = jnp.where(low, halves[:, 0], halves[:, 1])
    other = jnp.where(low, halves[:, 1], halves[:, 0])
    got = swapped(other.astype(jnp.bfloat16), "tp", 0)
    return mine + got.astype(jnp.float32)


def rms_normed(values, gain):
    square = jnp.mean(values * values, axis=-1, keepdims=True)
    return (values * lax.rsqrt(square + EPSILON) * gain).astype(jnp.bfloat16)


def rotate(vectors, positions):
    half = vectors.shape[-1] // 2
    exponent = jnp.arange(half, dtype=jnp.float32) * (-2.0 / vectors.shape[-1])
    freqs = jnp.power(jnp.float32(10000.0), exponent)
    angles = positions.astype(jnp.float32)[:, None] * freqs[None, :]
    cosine = jnp.cos(angles)[:, None, :]
    sine = jnp.sin(angles)[:, None, :]
    first = vectors[..., :half]
    second = vectors[..., half:]
    return jnp.concatenate(
        [first * cosine - second * sine, second * cosine + first * sine], axis=-1
    )


def partial_attention(query, keys, values, valid):
    scores = (
        jnp.einsum("pbcgd,pkcd->pbcgk", query, keys, preferred_element_type=jnp.float32) * 0.125
    )
    scores = jnp.where(valid, scores, SENTINEL)
    top = jnp.max(scores, axis=-1)
    weights = jnp.where(valid, jnp.exp(scores - top[..., None]), 0.0)
    total = jnp.sum(weights, axis=-1)
    weighted = jnp.einsum(
        "pbcgk,pkcd->pbcgd",
        weights.astype(jnp.bfloat16),
        values,
        preferred_element_type=jnp.float32,
    )
    return (weighted, top, total)


def on_device(
    tok_ids,
    accept,
    sub_ids,
    cache_len,
    spill,
    embed,
    attn_gain,
    w_query,
    w_key,
    w_value,
    w_out,
    mlp_gain,
    w_gate,
    w_up,
    w_down,
    cache_keys,
    cache_values,
):
    block = tok_ids.shape[0]
    slots = cache_keys.shape[0]
    query_local = w_query.shape[1] // HD
    stored_local = w_key.shape[1] // HD
    per_stored = query_local // stored_local
    group_index = lax.axis_index("grp")
    own_count = cache_len[group_index] - spill[group_index]
    far_count = spill[group_index]
    positions = cache_len[group_index] + jnp.arange(block, dtype=jnp.int32)
    slot_ids = jnp.arange(slots, dtype=jnp.int32)
    tail_ids = slot_ids[block:]
    store_keys = cache_keys.reshape(slots, stored_local, HD)
    store_values = cache_values.reshape(slots, stored_local, HD)
    second_ids = jnp.where(accept == 1, sub_ids, tok_ids)
    table = lax.all_gather(embed, "grp", axis=0, tiled=True)
    both_ids = jnp.concatenate([tok_ids, second_ids])
    x_part = jnp.take(table, both_ids, axis=0)
    rows, width = x_part.shape
    tail_keys, tail_values = swapped((cache_keys[block:], cache_values[block:]), "grp", 0)
    far_keys = tail_keys.reshape(slots - block, stored_local, HD)
    far_values = tail_values.reshape(slots - block, stored_local, HD)
    far_valid = tail_ids >= slots - far_count
    own_valid = slot_ids < own_count
    valid = jnp.concatenate([own_valid, far_valid, jnp.ones((block,), dtype=bool)])
    x_full = tp_gather(x_part)
    normed = rms_normed(x_full.astype(jnp.float32), attn_gain)
    both_positions = jnp.concatenate([positions, positions])
    query = rotate(
        jnp.dot(normed, w_query, preferred_element_type=jnp.float32).reshape(rows, query_local, HD),
        both_positions,
    )
    query = query.astype(jnp.bfloat16).reshape(2, block, stored_local, per_stored, HD)
    new_keys = (
        rotate(
            jnp.dot(normed, w_key, preferred_element_type=jnp.float32).reshape(
                rows, stored_local, HD
            ),
            both_positions,
        )
        .astype(jnp.bfloat16)
        .reshape(2, block, stored_local, HD)
    )
    new_values = (
        jnp.dot(normed, w_value, preferred_element_type=jnp.float32)
        .reshape(2, block, stored_local, HD)
        .astype(jnp.bfloat16)
    )
    cached_keys = jnp.concatenate([store_keys, far_keys], axis=0)
    cached_values = jnp.concatenate([store_values, far_values], axis=0)
    keys = jnp.concatenate(
        [jnp.broadcast_to(cached_keys[None], (2,) + cached_keys.shape), new_keys], axis=1
    )
    values = jnp.concatenate(
        [jnp.broadcast_to(cached_values[None], (2,) + cached_values.shape), new_values], axis=1
    )
    weighted, top, total = partial_attention(query, keys, values, valid)
    attended = weighted / total[..., None]
    mixed = attended.reshape(rows, query_local * HD).astype(jnp.bfloat16)
    head_term = jnp.dot(mixed, w_out, preferred_element_type=jnp.float32)
    head_sum = tp_reduce(head_term.astype(jnp.bfloat16))
    resid_part = (x_part.astype(jnp.float32) + head_sum).astype(jnp.bfloat16)
    resid_full = tp_gather(resid_part)
    normed_mlp = rms_normed(resid_full.astype(jnp.float32), mlp_gain)
    gate = jnp.dot(normed_mlp, w_gate, preferred_element_type=jnp.float32)
    lift = jnp.dot(normed_mlp, w_up, preferred_element_type=jnp.float32)
    hidden = (jax.nn.silu(gate) * lift).astype(jnp.bfloat16)
    down_term = jnp.dot(hidden, w_down, preferred_element_type=jnp.float32)
    down_part = tp_reduce(down_term.astype(jnp.bfloat16))
    out = (resid_part.astype(jnp.float32) + down_part).astype(jnp.bfloat16)
    return (out[:block], out[block:])


def solution(mesh):
    placed = (
        P("grp"),
        P("grp"),
        P("grp"),
        P(),
        P(),
        P("grp", "tp"),
        P(),
        P(None, "tp"),
        P(None, "tp"),
        P(None, "tp"),
        P("tp", None),
        P(),
        P(None, "tp"),
        P(None, "tp"),
        P("tp", None),
        P("grp", "tp"),
        P("grp", "tp"),
    )
    return jax.shard_map(
        on_device,
        mesh=mesh,
        in_specs=placed,
        out_specs=(P("grp", "tp"), P("grp", "tp")),
        check_vma=False,
    )
```

profile of v0, /device:TPU:32, one launch (start us, length us, event | category | flops | bytes accessed | tf_op | source)
XLA Modules:
  0.0 436.3 jit_solution(2578726305064428950)
XLA Ops:
  7.9 1.8 slice.43
  9.7 1.6 slice.45
  20.3 61.4 %all-gather.2.cloned.1.call-done = bf16[16384,256]{1,0:T(8,128)(2,1)} async-done(((bf16[512,256]{1,0:T(8,128)(2,1)}), bf16[16384,256]{1,0:T(8,128)(2,1)}) %all-gather.2.cloned.1.call-update) | async-done | bytes 8388624 | tf_op jit(solution)/shard_map/all_gather | solution.py:122
  81.7 6.0 %gather_fusion = bf16[512,256]{1,0:T(8,128)(2,1)S(1)} fusion(bf16[16384,256]{1,0:T(8,128)(2,1)} %all-gather.2.cloned.1.call-done, s32[1024]{0:T(1024)S(1)} %pad_clamp_fusion.1), kind=kCustom, calls=%fused_computation.2 | custom fusion | bytes 526336 | tf_op jit(solution)/shard_map/jit(_take)/gather | solution.py:124
  88.6 3.6 collective-permute-start.1
  93.4 2.3 copy.36
  96.8 10.1 %collective-permute-done.1 = bf16[512,256]{1,0:T(8,128)(2,1)} collective-permute-done((bf16[512,256]{1,0:T(8,128)(2,1)}, bf16[512,256]{1,0:T(8,128)(2,1)}, u32[]{:S(2)}, u32[]{:S(2)}) %collective-permute-start.1) | collective-permute-done | bytes 262176 | tf_op jit(solution)/shard_map/ppermute | solution.py:17
  108.1 3.1 collective-permute-start.3
  111.7 2.7 collective-permute-start.4
  114.4 1.8 maximum_bitcast_fusion.5
  117.2 7.4 %collective-permute-done.3 = bf16[2,512,256]{2,1,0:T(8,128)(2,1)S(1)} collective-permute-done((bf16[2,512,256]{2,1,0:T(8,128)(2,1)S(1)}, bf16[2,512,256]{2,1,0:T(8,128)(2,1)S(1)}, u32[]{:S(2)}, u32[]{:S(2)}) %collective-permute-start.3) | collective-permute-done | bytes 524320 | tf_op jit(solution)/shard_map/ppermute | solution.py:13
  124.6 9.6 %collective-permute-done.2 = bf16[2,512,256]{2,1,0:T(8,128)(2,1)S(1)} collective-permute-done((bf16[2,512,256]{2,1,0:T(8,128)(2,1)S(1)}, bf16[2,512,256]{2,1,0:T(8,128)(2,1)S(1)}, u32[]{:S(2)}, u32[]{:S(2)}) %collective-permute-start.2) | collective-permute-done | bytes 524320 | tf_op jit(solution)/shard_map/ppermute | solution.py:13
  134.2 1.6 pad_maximum_fusion
  135.8 3.7 gather_fusion.1
  139.5 2.4 fusion.10
  142.0 2.4 convert_bitcast_fusion
  144.3 5.7 %copy.32 = f32[512,4,2,256]{0,3,2,1:T(8,128)} copy(f32[512,4,2,256]{3,0,2,1:T(8,128)} %convert_bitcast_fusion) | data formatting | bytes 8388608 | tf_op jit(solution)/shard_map/convert_element_type | solution.py:133
  150.1 7.4 %copy.31 = f32[512,4,2,256]{3,2,1,0:T(2,128)} copy(f32[512,4,2,256]{3,0,2,1:T(8,128)} %convert_bitcast_fusion) | data formatting | bytes 8388608 | tf_op jit(solution)/shard_map/convert_element_type | solution.py:133
  158.1 3.6 fusion.18
  161.7 4.2 copy.35
  165.8 2.7 fusion.16
  170.1 6.4 %reshape.510 = f32[2,256,2048]{2,1,0:T(8,128)} reshape(f32[512,4,2,256]{3,2,1,0:T(2,128)} %copy.31) | data formatting | bytes 8388608 | tf_op jit(solution)/shard_map/convert_element_type | solution.py:133
  176.5 2.6 fusion.81
  179.4 12.5 %bitcast_reduce_fusion = (f32[2,256,4]{1,2,0:T(4,128)S(1)}, f32[2,4096,256,4]{2,1,3,0:T(8,128)}) fusion(pred[4096]{0:T(1024)(128)(4,1)S(1)} %pad_add_fusion, bf16[2,256,4,32]{1,3,2,0:T(8,128)(2,1)S(1)} %get-tuple-element.45, bf16[2,256,4,32]{1,3,2,0:T(8,128)(2,1)S(1)} %get-tuple-element.46, bf16[2,256,1,32]{1,3,0,2:T(8,128)(2,1)S(1)} %get-tuple-element.47, ...), kind=kOutput, calls=%fused_computation.4 | convolution fusion | flops 1102575616 | bytes 34877440 | tf_op jit(solution)/shard_map/pbcgd,pkcd->pbcgk/dot_general | solution.py:74
  191.9 15.6 %fusion.2 = f32[2,256,4]{1,2,0:T(4,128)S(1)} fusion(f32[2,4096,256,4]{2,1,3,0:T(8,128)} %get-tuple-element.44, f32[2,256,4]{1,2,0:T(4,128)S(1)} %get-tuple-element.43, pred[4096]{0:T(1024)(128)(4,1)S(1)} %pad_add_fusion), kind=kLoop, calls=%fused_computation.8 | loop fusion | flops 41940992 | bytes 33574912 | tf_op jit(solution)/shard_map/reduce_sum | solution.py:79
  208.4 15.7 %fusion.33 = bf16[2,256,1,4,64]{1,4,3,0,2:T(8,128)(2,1)S(1)} fusion(f32[2,4096,256,4]{2,1,3,0:T(8,128)} %get-tuple-element.44, f32[2,256,4]{1,2,0:T(4,128)S(1)} %get-tuple-element.43, pred[4096]{0:T(1024)(128)(4,1)S(1)} %pad_add_fusion, bf16[2,256,1,64]{1,3,0,2:T(8,128)(2,1)S(1)} %fusion.26, bf16[2,3840,1,64]{1,3,0,2:T(8,128)(2,1)S(1)} %broadcast_in_dim.78, ...), kind=kOutput, calls=%fused_computation.48 | convolution fusion | flops 1118044160 | bytes 34885632 | tf_op jit(solution)/shard_map/pbcgk,pkcd->pbcgd/dot_general | solution.py:80
  224.5 2.1 convolution_convert_fusion
  226.5 4.5 %reshape.399 = bf16[512,4,512]{2,1,0:T(4,128)(2,1)} reshape(bf16[512,2048]{1,0:T(8,128)(2,1)} %convolution_convert_fusion) | data formatting | bytes 4194304 | tf_op jit(solution)/shard_map/reshape | solution.py:40
  231.1 9.0 %constant_dynamic-slice_fusion.6 = (bf16[512,1,512]{2,1,0:T(2,128)(2,1)}, bf16[512,1,512]{2,1,0:T(2,128)(2,1)S(1)}, bf16[512,1,512]{2,1,0:T(2,128)(2,1)S(1)}, bf16[512,1,512]{2,1,0:T(2,128)(2,1)S(1)}) fusion(bf16[512,4,512]{2,1,0:T(4,128)(2,1)} %reshape.399, s32[]{:T(128)S(6)} %select_n.207, s32[]{:T(128)S(6)} %select_n.211, s32[]{:T(128)S(6)} %select_n.209, ...), kind=kLoop, calls=%fused_computation.136 | loop fusion | bytes 4194320 | tf_op jit(solution)/shard_map/jit(_take) | solution.py:41
  240.2 2.7 collective-permute-start.8
  244.7 1.5 collective-permute-start.7
  246.2 19.3 %collective-permute-done.8 = bf16[512,512]{1,0:T(8,128)(2,1)} collective-permute-done((bf16[512,512]{1,0:T(8,128)(2,1)S(1)}, bf16[512,512]{1,0:T(8,128)(2,1)}, u32[]{:S(2)}, u32[]{:S(2)}) %collective-permute-start.8) | collective-permute-done | bytes 524320 | tf_op jit(solution)/shard_map/ppermute | solution.py:13
  265.5 4.6 %collective-permute-done.6 = bf16[512,512]{1,0:T(8,128)(2,1)} collective-permute-done((bf16[512,512]{1,0:T(8,128)(2,1)}, bf16[512,512]{1,0:T(8,128)(2,1)}, u32[]{:S(2)}, u32[]{:S(2)}) %collective-permute-start.6) | collective-permute-done | bytes 524320 | tf_op jit(solution)/shard_map/ppermute | solution.py:13
  270.1 3.0 convert_add_fusion.1
  273.1 2.6 copy.46
  275.7 2.2 fusion.79
  277.9 1.2 copy.66
  279.2 2.1 copy.67
  282.3 2.6 collective-permute-start.9
  284.9 11.5 %collective-permute-done.9 = bf16[512,256]{1,0:T(8,128)(2,1)S(1)} collective-permute-done((bf16[512,256]{1,0:T(8,128)(2,1)S(1)}, bf16[512,256]{1,0:T(8,128)(2,1)S(1)}, u32[]{:S(2)}, u32[]{:S(2)}) %collective-permute-start.9) | collective-permute-done | bytes 262176 | tf_op jit(solution)/shard_map/ppermute | solution.py:17
  297.6 3.8 collective-permute-start.10
  301.4 9.2 %collective-permute-done.10 = bf16[512,256]{1,0:T(8,128)(2,1)S(1)} collective-permute-done((bf16[512,256]{1,0:T(8,128)(2,1)S(1)}, bf16[512,256]{1,0:T(8,128)(2,1)S(1)}, u32[]{:S(2)}, u32[]{:S(2)}) %collective-permute-start.10) | collective-permute-done | bytes 262176 | tf_op jit(solution)/shard_map/ppermute | solution.py:17
  311.7 3.4 collective-permute-start.13
  315.1 12.0 %collective-permute-done.12 = bf16[2,512,256]{2,1,0:T(8,128)(2,1)S(1)} collective-permute-done((bf16[2,512,256]{2,1,0:T(8,128)(2,1)S(1)}, bf16[2,512,256]{2,1,0:T(8,128)(2,1)S(1)}, u32[]{:S(2)}, u32[]{:S(2)}) %collective-permute-start.12) | collective-permute-done | bytes 524320 | tf_op jit(solution)/shard_map/ppermute | solution.py:13
  327.1 10.1 %collective-permute-done.11 = bf16[2,512,256]{2,1,0:T(8,128)(2,1)S(1)} collective-permute-done((bf16[2,512,256]{2,1,0:T(8,128)(2,1)S(1)}, bf16[2,512,256]{2,1,0:T(8,128)(2,1)S(1)}, u32[]{:S(2)}, u32[]{:S(2)}) %collective-permute-start.11) | collective-permute-done | bytes 524320 | tf_op jit(solution)/shard_map/ppermute | solution.py:13
  337.3 1.6 pad_maximum_fusion.1
  338.9 3.7 gather_fusion.2
  342.6 2.4 fusion.9
  345.1 2.3 convert_bitcast_fusion.1
  347.4 5.3 %copy.49 = f32[512,4,2,256]{0,3,2,1:T(8,128)} copy(f32[512,4,2,256]{3,0,2,1:T(8,128)} %convert_bitcast_fusion.1) | data formatting | bytes 8388608 | tf_op jit(solution)/shard_map/convert_element_type | solution.py:170
  352.7 2.8 fusion.14
  355.5 1.3 copy-done.6
  356.8 2.8 fusion.82
  359.6 7.6 %convolution_convert_fusion.1 = bf16[512,2048]{1,0:T(8,128)(2,1)} fusion(bf16[704,2048]{1,0:T(8,128)(2,1)S(1)} %copy-done, bf16[2048,704]{0,1:T(8,128)(2,1)} %param.34, bf16[512,2048]{0,1:T(8,128)(2,1)} %copy-done.6, f32[512,704]{0,1:T(8,128)} %fusion.82), kind=kOutput, calls=%fused_computation.31 | convolution fusion | flops 2956001280 | bytes 11403264 | tf_op jit(solution)/shard_map/dot_general | solution.py:174
  367.2 4.5 %reshape.401 = bf16[512,4,512]{2,1,0:T(4,128)(2,1)} reshape(bf16[512,2048]{1,0:T(8,128)(2,1)} %convolution_convert_fusion.1) | data formatting | bytes 4194304 | tf_op jit(solution)/shard_map/reshape | solution.py:40
  371.7 8.1 %constant_dynamic-slice_fusion.1 = (bf16[512,1,512]{2,1,0:T(2,128)(2,1)S(1)}, bf16[512,1,512]{2,1,0:T(2,128)(2,1)S(1)}, bf16[512,1,512]{2,1,0:T(2,128)(2,1)S(1)}, bf16[512,1,512]{2,1,0:T(2,128)(2,1)S(1)}) fusion(bf16[512,4,512]{2,1,0:T(4,128)(2,1)} %reshape.401, s32[]{:T(128)S(6)} %select_n.207, s32[]{:T(128)S(6)} %select_n.211, s32[]{:T(128)S(6)} %select_n.209, ...), kind=kLoop, calls=%fused_computation.131 | loop fusion | bytes 4194320 | tf_op jit(solution)/shard_map/jit(_take) | solution.py:41
  380.8 1.4 collective-permute-start.14
  383.1 11.9 %collective-permute-done.16 = bf16[512,512]{1,0:T(8,128)(2,1)S(1)} collective-permute-done((bf16[512,512]{1,0:T(8,128)(2,1)S(1)}, bf16[512,512]{1,0:T(8,128)(2,1)S(1)}, u32[]{:S(2)}, u32[]{:S(2)}) %collective-permute-start.16) | collective-permute-done | bytes 524320 | tf_op jit(solution)/shard_map/ppermute | solution.py:13
  395.0 11.6 %collective-permute-done.14 = bf16[512,512]{1,0:T(8,128)(2,1)S(1)} collective-permute-done((bf16[512,512]{1,0:T(8,128)(2,1)S(1)}, bf16[512,512]{1,0:T(8,128)(2,1)S(1)}, u32[]{:S(2)}, u32[]{:S(2)}) %collective-permute-start.14) | collective-permute-done | bytes 524320 | tf_op jit(solution)/shard_map/ppermute | solution.py:13
  406.6 1.3 convert_add_fusion
  407.9 2.6 copy.54
  410.5 2.2 fusion.78
  413.9 2.1 copy.73
  418.1 9.4 %collective-permute-done.17 = bf16[512,256]{1,0:T(8,128)(2,1)S(1)} collective-permute-done((bf16[512,256]{1,0:T(8,128)(2,1)S(1)}, bf16[512,256]{1,0:T(8,128)(2,1)S(1)}, u32[]{:S(2)}, u32[]{:S(2)}) %collective-permute-start.17) | collective-permute-done | bytes 262176 | tf_op jit(solution)/shard_map/ppermute | solution.py:17
  (115 shorter events, 29.4 us)
Async XLA Ops:
  7.2 352.4 %copy-start = (bf16[704,2048]{1,0:T(8,128)(2,1)S(1)}, bf16[704,2048]{1,0:T(8,128)(2,1)}, u32[]{:S(2)}) copy-start(bf16[704,2048]{1,0:T(8,128)(2,1)} %param.35) | copy-start | bytes 8650756
  7.2 85.6 %copy-start.15 = (f32[2048]{0:T(1024)S(1)}, f32[2048]{0:T(1024)}, u32[]{:S(2)}) copy-start(f32[2048]{0:T(1024)} %param.27) | copy-start | bytes 24580
  7.2 74.6 %all-gather.2.cloned.1.call-start = ((), (), s32[]{:S(2)}) async-start(), calls=%async_computation | async-start | bytes 8650752 | tf_op jit(solution)/shard_map/all_gather | solution.py:122
  9.7 106.5 %collective-permute-start = (bf16[1792,64]{0,1:T(8,128)(2,1)}, bf16[1792,64]{0,1:T(8,128)(2,1)}, u32[]{:S(2)}, u32[]{:S(2)}) collective-permute-start(bf16[1792,64]{0,1:T(8,128)(2,1)} %slice.43), channel_id=1, source_target_pairs={{0,8},{8,0},{16,24},{24,16},{32,40},{40,32},{48,56},{56,48},{64,72... | collective-permute-start | bytes 688136 | tf_op jit(solution)/shard_map/ppermute | solution.py:17
  11.3 103.0 %collective-permute-start.5 = (bf16[1792,64]{0,1:T(8,128)(2,1)}, bf16[1792,64]{0,1:T(8,128)(2,1)}, u32[]{:S(2)}, u32[]{:S(2)}) collective-permute-start(bf16[1792,64]{0,1:T(8,128)(2,1)} %slice.45), channel_id=1, source_target_pairs={{0,8},{8,0},{16,24},{24,16},{32,40},{40,32},{48,56},{56,48},{64,72... | collective-permute-start | bytes 688136 | tf_op jit(solution)/shard_map/ppermute | solution.py:17
  18.3 74.5 %copy-start.19 = (pred[512]{0:T(512)(128)(4,1)}, pred[512]{0:T(512)(128)(4,1)S(1)}, u32[]{:S(2)}) copy-start(pred[512]{0:T(512)(128)(4,1)S(1)} %compare_and_fusion.1) | copy-start | bytes 1540
  87.8 20.3 %copy-start.4 = (bf16[512,256]{1,0:T(8,128)(2,1)}, bf16[512,256]{1,0:T(8,128)(2,1)S(1)}, u32[]{:S(2)}) copy-start(bf16[512,256]{1,0:T(8,128)(2,1)S(1)} %gather_fusion) | copy-start | bytes 786436
  88.6 18.3 %collective-permute-start.1 = (bf16[512,256]{1,0:T(8,128)(2,1)}, bf16[512,256]{1,0:T(8,128)(2,1)}, u32[]{:S(2)}, u32[]{:S(2)}) collective-permute-start(bf16[512,256]{1,0:T(8,128)(2,1)} %broadcast_select_fusion.2), channel_id=1, source_target_pairs={{0,1},{1,0},{2,3},{3,2},{4,5},{5,4},{6,7},{7,6},{8,9},{9,8},{10,11... | collective-permute-start | bytes 786440 | tf_op jit(solution)/shard_map/ppermute | solution.py:17
  93.4 21.0 %copy-start.9 = (bf16[2048,64]{0,1:T(8,128)(2,1)S(1)}, bf16[2048,64]{0,1:T(8,128)(2,1)}, u32[]{:S(2)}) copy-start(bf16[2048,64]{0,1:T(8,128)(2,1)} %param.36) | copy-start | bytes 786436
  95.8 20.4 %copy-start.10 = (bf16[2048,64]{0,1:T(8,128)(2,1)S(1)}, bf16[2048,64]{0,1:T(8,128)(2,1)}, u32[]{:S(2)}) copy-start(bf16[2048,64]{0,1:T(8,128)(2,1)} %param.37) | copy-start | bytes 786436
  108.1 16.5 %collective-permute-start.3 = (bf16[2,512,256]{2,1,0:T(8,128)(2,1)S(1)}, bf16[2,512,256]{2,1,0:T(8,128)(2,1)S(1)}, u32[]{:S(2)}, u32[]{:S(2)}) collective-permute-start(bf16[2,512,256]{2,1,0:T(8,128)(2,1)S(1)} %get-tuple-element.34), channel_id=1, source_target_pairs={{0,4},{1,5},{2,6},{3,7},{4,0},{5,1},{6,2},{7,3},{8,12},{9,13},{10,... | collective-permute-start | bytes 1572872 | tf_op jit(solution)/shard_map/ppermute | solution.py:13
  111.2 23.0 %collective-permute-start.2 = (bf16[2,512,256]{2,1,0:T(8,128)(2,1)S(1)}, bf16[2,512,256]{2,1,0:T(8,128)(2,1)S(1)}, u32[]{:S(2)}, u32[]{:S(2)}) collective-permute-start(bf16[2,512,256]{2,1,0:T(8,128)(2,1)S(1)} %get-tuple-element.34), channel_id=1, source_target_pairs={{0,2},{1,3},{2,4},{3,5},{4,6},{5,7},{6,0},{7,1},{8,10},{9,11},{10,... | collective-permute-start | bytes 1572872 | tf_op jit(solution)/shard_map/ppermute | solution.py:13
  111.7 22.5 %collective-permute-start.4 = (bf16[2,512,256]{2,1,0:T(8,128)(2,1)S(1)}, bf16[2,512,256]{2,1,0:T(8,128)(2,1)S(1)}, u32[]{:S(2)}, u32[]{:S(2)}) collective-permute-start(bf16[2,512,256]{2,1,0:T(8,128)(2,1)S(1)} %get-tuple-element.34), channel_id=1, source_target_pairs={{0,6},{1,7},{2,0},{3,1},{4,2},{5,3},{6,4},{7,5},{8,14},{9,15},{10,... | collective-permute-start | bytes 1572872 | tf_op jit(solution)/shard_map/ppermute | solution.py:13
  135.8 3.7 copy-start.17
  139.5 2.4 copy-start.1
  150.1 8.0 %copy-start.16 = (f32[4,2,256]{2,1,0:T(2,128)S(1)}, f32[4,2,256]{2,1,0:T(2,128)}, u32[]{:S(2)}) copy-start(f32[4,2,256]{2,1,0:T(2,128)} %mul.193) | copy-start | bytes 24580
  165.8 2.7 copy-start.11
  168.5 0.7 copy-start.23
  176.5 2.7 copy-start.13
  176.5 2.7 copy-start.14
  176.5 2.8 copy-start.7
  191.9 15.6 %copy-start.3 = (f32[2,256,2048]{2,1,0:T(8,128)S(1)}, f32[2,256,2048]{2,1,0:T(8,128)}, u32[]{:S(2)}) copy-start(f32[2,256,2048]{2,1,0:T(8,128)} %reshape.510) | copy-start | bytes 12582916
  191.9 15.6 %copy-start.12 = (bf16[2048,64]{0,1:T(8,128)(2,1)S(1)}, bf16[2048,64]{0,1:T(8,128)(2,1)}, u32[]{:S(2)}) copy-start(bf16[2048,64]{0,1:T(8,128)(2,1)} %param.30) | copy-start | bytes 786436
  191.9 15.6 %copy-start.22 = (f32[2,256]{1,0:T(2,128)S(1)}, f32[2,256]{1,0:T(2,128)}, u32[]{:S(2)}) copy-start(f32[2,256]{1,0:T(2,128)} %rsqrt.21) | copy-start | bytes 6148
  208.4 16.0 %copy-start.8 = (bf16[256,2048]{1,0:T(8,128)(2,1)S(1)}, bf16[256,2048]{1,0:T(8,128)(2,1)}, u32[]{:S(2)}) copy-start(bf16[256,2048]{1,0:T(8,128)(2,1)} %param.31) | copy-start | bytes 3145732
  240.2 25.3 %collective-permute-start.8 = (bf16[512,512]{1,0:T(8,128)(2,1)S(1)}, bf16[512,512]{1,0:T(8,128)(2,1)}, u32[]{:S(2)}, u32[]{:S(2)}) collective-permute-start(bf16[512,512]{1,0:T(8,128)(2,1)S(1)} %fusion.47), channel_id=1, source_target_pairs={{0,6},{1,7},{2,0},{3,1},{4,2},{5,3},{6,4},{7,5},{8,14},{9,15},{10,... | collective-permute-start | bytes 1572872 | tf_op jit(solution)/shard_map/ppermute | solution.py:13
  243.8 26.3 %collective-permute-start.6 = (bf16[512,512]{1,0:T(8,128)(2,1)}, bf16[512,512]{1,0:T(8,128)(2,1)}, u32[]{:S(2)}, u32[]{:S(2)}) collective-permute-start(bf16[512,512]{1,0:T(8,128)(2,1)} %fusion.49), channel_id=1, source_target_pairs={{0,2},{1,3},{2,4},{3,5},{4,6},{5,7},{6,0},{7,1},{8,10},{9,11},{10,... | collective-permute-start | bytes 1572872 | tf_op jit(solution)/shard_map/ppermute | solution.py:13
  244.7 25.4 %collective-permute-start.7 = (bf16[512,512]{1,0:T(8,128)(2,1)}, bf16[512,512]{1,0:T(8,128)(2,1)}, u32[]{:S(2)}, u32[]{:S(2)}) collective-permute-start(bf16[512,512]{1,0:T(8,128)(2,1)} %fusion.48), channel_id=1, source_target_pairs={{0,4},{1,5},{2,6},{3,7},{4,0},{5,1},{6,2},{7,3},{8,12},{9,13},{10,... | collective-permute-start | bytes 1572872 | tf_op jit(solution)/shard_map/ppermute | solution.py:13
  277.9 18.5 %copy-start.20 = (pred[512]{0:T(512)(128)(4,1)S(1)}, pred[512]{0:T(512)(128)(4,1)}, u32[]{:S(2)}) copy-start(pred[512]{0:T(512)(128)(4,1)} %copy-done.19) | copy-start | bytes 1540
  282.3 14.1 %collective-permute-start.9 = (bf16[512,256]{1,0:T(8,128)(2,1)S(1)}, bf16[512,256]{1,0:T(8,128)(2,1)S(1)}, u32[]{:S(2)}, u32[]{:S(2)}) collective-permute-start(bf16[512,256]{1,0:T(8,128)(2,1)S(1)} %fusion.55), channel_id=1, source_target_pairs={{0,1},{1,0},{2,3},{3,2},{4,5},{5,4},{6,7},{7,6},{8,9},{9,8},{10,11... | collective-permute-start | bytes 786440 | tf_op jit(solution)/shard_map/ppermute | solution.py:17
  297.6 13.0 %copy-start.5 = (bf16[512,256]{1,0:T(8,128)(2,1)}, bf16[512,256]{1,0:T(8,128)(2,1)S(1)}, u32[]{:S(2)}) copy-start(bf16[512,256]{1,0:T(8,128)(2,1)S(1)} %fusion.54) | copy-start | bytes 786436
  297.6 13.0 %collective-permute-start.10 = (bf16[512,256]{1,0:T(8,128)(2,1)S(1)}, bf16[512,256]{1,0:T(8,128)(2,1)S(1)}, u32[]{:S(2)}, u32[]{:S(2)}) collective-permute-start(bf16[512,256]{1,0:T(8,128)(2,1)S(1)} %fusion.54), channel_id=1, source_target_pairs={{0,1},{1,0},{2,3},{3,2},{4,5},{5,4},{6,7},{7,6},{8,9},{9,8},{10,11... | collective-permute-start | bytes 786440 | tf_op jit(solution)/shard_map/ppermute | solution.py:17
  310.7 16.4 %collective-permute-start.12 = (bf16[2,512,256]{2,1,0:T(8,128)(2,1)S(1)}, bf16[2,512,256]{2,1,0:T(8,128)(2,1)S(1)}, u32[]{:S(2)}, u32[]{:S(2)}) collective-permute-start(bf16[2,512,256]{2,1,0:T(8,128)(2,1)S(1)} %get-tuple-element.30), channel_id=1, source_target_pairs={{0,4},{1,5},{2,6},{3,7},{4,0},{5,1},{6,2},{7,3},{8,12},{9,13},{10,... | collective-permute-start | bytes 1572872 | tf_op jit(solution)/shard_map/ppermute | solution.py:13
  311.7 25.6 %collective-permute-start.11 = (bf16[2,512,256]{2,1,0:T(8,128)(2,1)S(1)}, bf16[2,512,256]{2,1,0:T(8,128)(2,1)S(1)}, u32[]{:S(2)}, u32[]{:S(2)}) collective-permute-start(bf16[2,512,256]{2,1,0:T(8,128)(2,1)S(1)} %get-tuple-element.30), channel_id=1, source_target_pairs={{0,2},{1,3},{2,4},{3,5},{4,6},{5,7},{6,0},{7,1},{8,10},{9,11},{10,... | collective-permute-start | bytes 1572872 | tf_op jit(solution)/shard_map/ppermute | solution.py:13
  311.7 25.6 %collective-permute-start.13 = (bf16[2,512,256]{2,1,0:T(8,128)(2,1)S(1)}, bf16[2,512,256]{2,1,0:T(8,128)(2,1)S(1)}, u32[]{:S(2)}, u32[]{:S(2)}) collective-permute-start(bf16[2,512,256]{2,1,0:T(8,128)(2,1)S(1)} %get-tuple-element.30), channel_id=1, source_target_pairs={{0,6},{1,7},{2,0},{3,1},{4,2},{5,3},{6,4},{7,5},{8,14},{9,15},{10,... | collective-permute-start | bytes 1572872 | tf_op jit(solution)/shard_map/ppermute | solution.py:13
  338.9 3.7 copy-start.18
  342.6 2.4 copy-start.2
  347.4 5.3 %copy-start.21 = (f32[2048]{0:T(1024)S(1)}, f32[2048]{0:T(1024)}, u32[]{:S(2)}) copy-start(f32[2048]{0:T(1024)} %param.32) | copy-start | bytes 24580
  352.7 4.1 copy-start.24
  355.5 1.3 copy-start.6
  380.1 14.9 %collective-permute-start.16 = (bf16[512,512]{1,0:T(8,128)(2,1)S(1)}, bf16[512,512]{1,0:T(8,128)(2,1)S(1)}, u32[]{:S(2)}, u32[]{:S(2)}) collective-permute-start(bf16[512,512]{1,0:T(8,128)(2,1)S(1)} %fusion.43), channel_id=1, source_target_pairs={{0,6},{1,7},{2,0},{3,1},{4,2},{5,3},{6,4},{7,5},{8,14},{9,15},{10,... | collective-permute-start | bytes 1572872 | tf_op jit(solution)/shard_map/ppermute | solution.py:13
  380.8 25.8 %collective-permute-start.14 = (bf16[512,512]{1,0:T(8,128)(2,1)S(1)}, bf16[512,512]{1,0:T(8,128)(2,1)S(1)}, u32[]{:S(2)}, u32[]{:S(2)}) collective-permute-start(bf16[512,512]{1,0:T(8,128)(2,1)S(1)} %fusion.45), channel_id=1, source_target_pairs={{0,2},{1,3},{2,4},{3,5},{4,6},{5,7},{6,0},{7,1},{8,10},{9,11},{10,... | collective-permute-start | bytes 1572872 | tf_op jit(solution)/shard_map/ppermute | solution.py:13
  382.2 24.4 %collective-permute-start.15 = (bf16[512,512]{1,0:T(8,128)(2,1)S(1)}, bf16[512,512]{1,0:T(8,128)(2,1)S(1)}, u32[]{:S(2)}, u32[]{:S(2)}) collective-permute-start(bf16[512,512]{1,0:T(8,128)(2,1)S(1)} %fusion.44), channel_id=1, source_target_pairs={{0,4},{1,5},{2,6},{3,7},{4,0},{5,1},{6,2},{7,3},{8,12},{9,13},{10,... | collective-permute-start | bytes 1572872 | tf_op jit(solution)/shard_map/ppermute | solution.py:13
  417.1 10.4 %collective-permute-start.17 = (bf16[512,256]{1,0:T(8,128)(2,1)S(1)}, bf16[512,256]{1,0:T(8,128)(2,1)S(1)}, u32[]{:S(2)}, u32[]{:S(2)}) collective-permute-start(bf16[512,256]{1,0:T(8,128)(2,1)S(1)} %fusion.56), channel_id=1, source_target_pairs={{0,1},{1,0},{2,3},{3,2},{4,5},{5,4},{6,7},{7,6},{8,9},{9,8},{10,11... | collective-permute-start | bytes 786440 | tf_op jit(solution)/shard_map/ppermute | solution.py:17
Sparse Core Ops, SparseCore 0:
  9.9 71.8 all-gather.1
where the time goes:
time: 444 us; the launch traced here: 436 us
  waiting for transfers between devices  189 us (43%)
  local copies, waits for them, and re-layouts  97 us (22%)
  other arithmetic  59.6 us (13%)
  matrix products  44.6 us (10%)
  starting transfers between devices  29.5 us (7%)
  between operations  16.6 us (4%)
    ppermute x12, waiting for transfers between devices, shifted(): return lax.ppermute(array, axis, [(i, (i + step) % n) for i in range(n)])  86.6 us
    all_gather x1, waiting for transfers between devices, on_device(): table = lax.all_gather(embed, 'grp', axis=0, tiled=True)  61.4 us
    ppermute x6, waiting for transfers between devices, swapped(): lax.ppermute(array, axis, [(i, i ^ 1 << bit) for i in range(lax.axis_size...  40.3 us
    convert_element_type x3, local copies, waits for them, and re-layouts, on_device(): normed = rms_normed(x_full.astype(jnp.float32), attn_gain)  19.5 us
    ppermute x12, starting transfers between devices, shifted(): return lax.ppermute(array, axis, [(i, (i + step) % n) for i in range(n)])  17.9 us
    another operation x2, local copies, waits for them, and re-layouts, tp_reduce(): acc = jnp.take(pieces, mine_x, axis=1).astype(jnp.float32)  17.1 us
    dot_general x1, matrix products, partial_attention(): jnp.einsum('pbcgk,pkcd->pbcgd', weights.astype(jnp.bfloat16), values, pre...  15.7 us
    reduce_sum x1, other arithmetic, partial_attention(): total = jnp.sum(weights, axis=-1)  15.6 us
  transfers between devices with their start and end apart: 19, of which 14 were waited for; matrix products, arithmetic and copies ran while one was open for 6% of the time, Pallas kernels for 0%

commit v1 on v0

--- a/solution.py
+++ b/solution.py
@@ -119,7 +119,9 @@
     store_keys = cache_keys.reshape(slots, stored_local, HD)
     store_values = cache_values.reshape(slots, stored_local, HD)
     second_ids = jnp.where(accept == 1, sub_ids, tok_ids)
-    table = lax.all_gather(embed, "grp", axis=0, tiled=True)
+    table = jnp.concatenate(
+        lax.all_to_all(jnp.stack([embed] * lax.axis_size("grp")), "grp", 0, 0), axis=0
+    )
     both_ids = jnp.concatenate([tok_ids, second_ids])
     x_part = jnp.take(table, both_ids, axis=0)
     rows, width = x_part.shape

time: 444 us -> 553 us (1.25)
  the two profiles are of different devices: /device:TPU:32 before, /device:TPU:24 now
where the time goes in v1:
time: 553 us; the launch traced here: 545 us
  waiting for transfers between devices  300 us (54%)
  local copies, waits for them, and re-layouts  98.9 us (18%)
  other arithmetic  57.6 us (10%)
  matrix products  44.7 us (8%)
  starting transfers between devices  40.8 us (7%)
    all_to_all x1, waiting for transfers between devices, on_device(): lax.all_to_all(jnp.stack([embed] * lax.axis_size('grp')), 'grp', 0, 0)  176 us
    ppermute x12, waiting for transfers between devices, shifted(): return lax.ppermute(array, axis, [(i, (i + step) % n) for i in range(n)])  85.5 us
    ppermute x6, waiting for transfers between devices, swapped(): lax.ppermute(array, axis, [(i, i ^ 1 << bit) for i in range(lax.axis_size...  37.7 us
    convert_element_type x3, local copies, waits for them, and re-layouts, on_device(): normed = rms_normed(x_full.astype(jnp.float32), attn_gain)  19.6 us
    ppermute x12, starting transfers between devices, shifted(): return lax.ppermute(array, axis, [(i, (i + step) % n) for i in range(n)])  17.9 us
    another operation x2, local copies, waits for them, and re-layouts, tp_reduce(): acc = jnp.take(pieces, mine_x, axis=1).astype(jnp.float32)  17 us
    dot_general x1, matrix products, partial_attention(): jnp.einsum('pbcgk,pkcd->pbcgd', weights.astype(jnp.bfloat16), values, pre...  15.7 us
    reduce_sum x1, other arithmetic, partial_attention(): total = jnp.sum(weights, axis=-1)  15.6 us
  transfers between devices with their start and end apart: 19, of which 14 were waited for; matrix products, arithmetic and copies ran while one was open for 4% of the time, Pallas kernels for 0%

profile of v1, /device:TPU:24, one launch (start us, length us, event | category | flops | bytes accessed | tf_op | source)
XLA Modules:
  0.0 544.9 jit_solution(3738768196180666298)
XLA Ops:
  0.6 5.3 stack.34
  6.0 9.1 %all-to-all-start = ((bf16[32,512,256]{2,1,0:T(8,128)(2,1)}), bf16[32,512,256]{2,1,0:T(8,128)(2,1)}, u32[]{:S(2)}, u32[]{:S(2)}) async-start(bf16[32,512,256]{2,1,0:T(8,128)(2,1)} %stack.34), calls=%async_computation | async-start | bytes 16777216 | tf_op jit(solution)/shard_map/all_to_all | solution.py:123
  22.3 176.4 %all-to-all-done = bf16[32,512,256]{2,1,0:T(8,128)(2,1)} async-done(((bf16[32,512,256]{2,1,0:T(8,128)(2,1)}), bf16[32,512,256]{2,1,0:T(8,128)(2,1)}, u32[]{:S(2)}, u32[]{:S(2)}) %all-to-all-start) | async-done | bytes 8388640 | tf_op jit(solution)/shard_map/all_to_all | solution.py:123
  198.7 6.0 %gather_fusion = bf16[512,256]{1,0:T(8,128)(2,1)S(1)} fusion(bf16[16384,256]{1,0:T(8,128)(2,1)} %bitcast, s32[1024]{0:T(1024)S(1)} %pad_clamp_fusion.1), kind=kCustom, calls=%fused_computation.2 | custom fusion | bytes 526336 | tf_op jit(solution)/shard_map/jit(_take)/gather | solution.py:126
  205.6 4.5 collective-permute-start.1
  211.2 2.3 copy.36
  214.5 9.2 %collective-permute-done.1 = bf16[512,256]{1,0:T(8,128)(2,1)} collective-permute-done((bf16[512,256]{1,0:T(8,128)(2,1)}, bf16[512,256]{1,0:T(8,128)(2,1)}, u32[]{:S(2)}, u32[]{:S(2)}) %collective-permute-start.1) | collective-permute-done | bytes 262176 | tf_op jit(solution)/shard_map/ppermute | solution.py:17
  224.9 3.1 collective-permute-start.3
  228.6 2.6 collective-permute-start.4
  231.3 1.8 maximum_bitcast_fusion.5
  234.0 7.4 %collective-permute-done.3 = bf16[2,512,256]{2,1,0:T(8,128)(2,1)S(1)} collective-permute-done((bf16[2,512,256]{2,1,0:T(8,128)(2,1)S(1)}, bf16[2,512,256]{2,1,0:T(8,128)(2,1)S(1)}, u32[]{:S(2)}, u32[]{:S(2)}) %collective-permute-start.3) | collective-permute-done | bytes 524320 | tf_op jit(solution)/shard_map/ppermute | solution.py:13
  241.4 9.2 %collective-permute-done.2 = bf16[2,512,256]{2,1,0:T(8,128)(2,1)S(1)} collective-permute-done((bf16[2,512,256]{2,1,0:T(8,128)(2,1)S(1)}, bf16[2,512,256]{2,1,0:T(8,128)(2,1)S(1)}, u32[]{:S(2)}, u32[]{:S(2)}) %collective-permute-start.2) | collective-permute-done | bytes 524320 | tf_op jit(solution)/shard_map/ppermute | solution.py:13
  250.8 1.6 pad_maximum_fusion
  252.4 3.7 gather_fusion.1
  256.1 2.4 fusion.10
  258.5 2.4 convert_bitcast_fusion
  260.9 5.7 %copy.32 = f32[512,4,2,256]{0,3,2,1:T(8,128)} copy(f32[512,4,2,256]{3,0,2,1:T(8,128)} %convert_bitcast_fusion) | data formatting | bytes 8388608 | tf_op jit(solution)/shard_map/convert_element_type | solution.py:135
  266.7 7.4 %copy.31 = f32[512,4,2,256]{3,2,1,0:T(2,128)} copy(f32[512,4,2,256]{3,0,2,1:T(8,128)} %convert_bitcast_fusion) | data formatting | bytes 8388608 | tf_op jit(solution)/shard_map/convert_element_type | solution.py:135
  274.7 3.6 fusion.18
  278.3 4.1 copy.35
  282.4 2.7 fusion.16
  286.7 6.4 %reshape.516 = f32[2,256,2048]{2,1,0:T(8,128)} reshape(f32[512,4,2,256]{3,2,1,0:T(2,128)} %copy.31) | data formatting | bytes 8388608 | tf_op jit(solution)/shard_map/convert_element_type | solution.py:135
  293.1 2.6 fusion.81
  296.0 12.6 %bitcast_reduce_fusion = (f32[2,256,4]{1,2,0:T(4,128)S(1)}, f32[2,4096,256,4]{2,1,3,0:T(8,128)}) fusion(pred[4096]{0:T(1024)(128)(4,1)S(1)} %pad_add_fusion, bf16[2,256,4,32]{1,3,2,0:T(8,128)(2,1)S(1)} %get-tuple-element.45, bf16[2,256,4,32]{1,3,2,0:T(8,128)(2,1)S(1)} %get-tuple-element.46, bf16[2,256,1,32]{1,3,0,2:T(8,128)(2,1)S(1)} %get-tuple-element.47, ...), kind=kOutput, calls=%fused_computation.4 | convolution fusion | flops 1102575616 | bytes 34877440 | tf_op jit(solution)/shard_map/pbcgd,pkcd->pbcgk/dot_general | solution.py:74
  308.5 15.6 %fusion.2 = f32[2,256,4]{1,2,0:T(4,128)S(1)} fusion(f32[2,4096,256,4]{2,1,3,0:T(8,128)} %get-tuple-element.44, f32[2,256,4]{1,2,0:T(4,128)S(1)} %get-tuple-element.43, pred[4096]{0:T(1024)(128)(4,1)S(1)} %pad_add_fusion), kind=kLoop, calls=%fused_computation.8 | loop fusion | flops 41940992 | bytes 33574912 | tf_op jit(solution)/shard_map/reduce_sum | solution.py:79
  325.1 15.7 %fusion.33 = bf16[2,256,1,4,64]{1,4,3,0,2:T(8,128)(2,1)S(1)} fusion(f32[2,4096,256,4]{2,1,3,0:T(8,128)} %get-tuple-element.44, f32[2,256,4]{1,2,0:T(4,128)S(1)} %get-tuple-element.43, pred[4096]{0:T(1024)(128)(4,1)S(1)} %pad_add_fusion, bf16[2,256,1,64]{1,3,0,2:T(8,128)(2,1)S(1)} %fusion.26, bf16[2,3840,1,64]{1,3,0,2:T(8,128)(2,1)S(1)} %broadcast_in_dim.78, ...), kind=kOutput, calls=%fused_computation.48 | convolution fusion | flops 1118044160 | bytes 34885632 | tf_op jit(solution)/shard_map/pbcgk,pkcd->pbcgd/dot_general | solution.py:80
  341.1 2.1 convolution_convert_fusion
  343.2 4.5 reshape.405
  347.7 8.9 %constant_dynamic-slice_fusion.6 = (bf16[512,1,512]{2,1,0:T(2,128)(2,1)}, bf16[512,1,512]{2,1,0:T(2,128)(2,1)S(1)}, bf16[512,1,512]{2,1,0:T(2,128)(2,1)S(1)}, bf16[512,1,512]{2,1,0:T(2,128)(2,1)S(1)}) fusion(bf16[512,4,512]{2,1,0:T(4,128)(2,1)} %reshape.405, s32[]{:T(128)S(6)} %select_n.207, s32[]{:T(128)S(6)} %select_n.211, s32[]{:T(128)S(6)} %select_n.209, ...), kind=kLoop, calls=%fused_computation.136 | loop fusion | bytes 4194320 | tf_op jit(solution)/shard_map/jit(_take) | solution.py:41
  356.7 2.7 collective-permute-start.8
  361.2 1.5 collective-permute-start.7
  362.7 19.4 %collective-permute-done.8 = bf16[512,512]{1,0:T(8,128)(2,1)} collective-permute-done((bf16[512,512]{1,0:T(8,128)(2,1)S(1)}, bf16[512,512]{1,0:T(8,128)(2,1)}, u32[]{:S(2)}, u32[]{:S(2)}) %collective-permute-start.8) | collective-permute-done | bytes 524320 | tf_op jit(solution)/shard_map/ppermute | solution.py:13
  382.0 4.6 collective-permute-done.6
  386.6 3.0 convert_add_fusion.1
  389.7 2.5 copy.46
  392.2 2.2 fusion.79
  395.7 2.0 copy.67
  398.8 3.1 collective-permute-start.9
  401.9 11.5 %collective-permute-done.9 = bf16[512,256]{1,0:T(8,128)(2,1)S(1)} collective-permute-done((bf16[512,256]{1,0:T(8,128)(2,1)S(1)}, bf16[512,256]{1,0:T(8,128)(2,1)S(1)}, u32[]{:S(2)}, u32[]{:S(2)}) %collective-permute-start.9) | collective-permute-done | bytes 262176 | tf_op jit(solution)/shard_map/ppermute | solution.py:17
  414.6 2.7 collective-permute-start.10
  417.2 9.5 %collective-permute-done.10 = bf16[512,256]{1,0:T(8,128)(2,1)S(1)} collective-permute-done((bf16[512,256]{1,0:T(8,128)(2,1)S(1)}, bf16[512,256]{1,0:T(8,128)(2,1)S(1)}, u32[]{:S(2)}, u32[]{:S(2)}) %collective-permute-start.10) | collective-permute-done | bytes 262176 | tf_op jit(solution)/shard_map/ppermute | solution.py:17
  427.8 3.4 collective-permute-start.13
  431.2 12.1 %collective-permute-done.12 = bf16[2,512,256]{2,1,0:T(8,128)(2,1)S(1)} collective-permute-done((bf16[2,512,256]{2,1,0:T(8,128)(2,1)S(1)}, bf16[2,512,256]{2,1,0:T(8,128)(2,1)S(1)}, u32[]{:S(2)}, u32[]{:S(2)}) %collective-permute-start.12) | collective-permute-done | bytes 524320 | tf_op jit(solution)/shard_map/ppermute | solution.py:13
  443.3 9.2 %collective-permute-done.11 = bf16[2,512,256]{2,1,0:T(8,128)(2,1)S(1)} collective-permute-done((bf16[2,512,256]{2,1,0:T(8,128)(2,1)S(1)}, bf16[2,512,256]{2,1,0:T(8,128)(2,1)S(1)}, u32[]{:S(2)}, u32[]{:S(2)}) %collective-permute-start.11) | collective-permute-done | bytes 524320 | tf_op jit(solution)/shard_map/ppermute | solution.py:13
  452.5 1.6 pad_maximum_fusion.1
  454.2 3.7 gather_fusion.2
  457.9 2.4 fusion.9
  460.3 2.3 convert_bitcast_fusion.1
  462.7 5.3 copy.49
  468.0 2.8 fusion.14
  470.8 1.4 copy-done.6
  472.1 2.8 fusion.82
  474.9 7.6 %convolution_convert_fusion.1 = bf16[512,2048]{1,0:T(8,128)(2,1)} fusion(bf16[704,2048]{1,0:T(8,128)(2,1)S(1)} %copy-done, bf16[2048,704]{0,1:T(8,128)(2,1)} %param.34, bf16[512,2048]{0,1:T(8,128)(2,1)} %copy-done.6, f32[512,704]{0,1:T(8,128)} %fusion.82), kind=kOutput, calls=%fused_computation.31 | convolution fusion | flops 2956001280 | bytes 11403264 | tf_op jit(solution)/shard_map/dot_general | solution.py:176
  482.5 4.5 reshape.407
  487.1 8.1 %constant_dynamic-slice_fusion.1 = (bf16[512,1,512]{2,1,0:T(2,128)(2,1)S(1)}, bf16[512,1,512]{2,1,0:T(2,128)(2,1)S(1)}, bf16[512,1,512]{2,1,0:T(2,128)(2,1)S(1)}, bf16[512,1,512]{2,1,0:T(2,128)(2,1)S(1)}) fusion(bf16[512,4,512]{2,1,0:T(4,128)(2,1)} %reshape.407, s32[]{:T(128)S(6)} %select_n.207, s32[]{:T(128)S(6)} %select_n.211, s32[]{:T(128)S(6)} %select_n.209, ...), kind=kLoop, calls=%fused_computation.131 | loop fusion | bytes 4194320 | tf_op jit(solution)/shard_map/jit(_take) | solution.py:41
  496.2 1.4 collective-permute-start.14
  498.5 11.9 %collective-permute-done.16 = bf16[512,512]{1,0:T(8,128)(2,1)S(1)} collective-permute-done((bf16[512,512]{1,0:T(8,128)(2,1)S(1)}, bf16[512,512]{1,0:T(8,128)(2,1)S(1)}, u32[]{:S(2)}, u32[]{:S(2)}) %collective-permute-start.16) | collective-permute-done | bytes 524320 | tf_op jit(solution)/shard_map/ppermute | solution.py:13
  510.3 11.6 %collective-permute-done.14 = bf16[512,512]{1,0:T(8,128)(2,1)S(1)} collective-permute-done((bf16[512,512]{1,0:T(8,128)(2,1)S(1)}, bf16[512,512]{1,0:T(8,128)(2,1)S(1)}, u32[]{:S(2)}, u32[]{:S(2)}) %collective-permute-start.14) | collective-permute-done | bytes 524320 | tf_op jit(solution)/shard_map/ppermute | solution.py:13
  521.9 1.3 convert_add_fusion
  523.2 2.6 copy.54
  525.8 2.2 fusion.78
  529.3 2.0 copy.73
  532.4 3.0 collective-permute-start.17
  535.4 7.5 %collective-permute-done.17 = bf16[512,256]{1,0:T(8,128)(2,1)S(1)} collective-permute-done((bf16[512,256]{1,0:T(8,128)(2,1)S(1)}, bf16[512,256]{1,0:T(8,128)(2,1)S(1)}, u32[]{:S(2)}, u32[]{:S(2)}) %collective-permute-start.17) | collective-permute-done | bytes 262176 | tf_op jit(solution)/shard_map/ppermute | solution.py:17
  (127 shorter events, 27.0 us)
Async XLA Ops:
  0.6 474.3 %copy-start = (bf16[704,2048]{1,0:T(8,128)(2,1)S(1)}, bf16[704,2048]{1,0:T(8,128)(2,1)}, u32[]{:S(2)}) copy-start(bf16[704,2048]{1,0:T(8,128)(2,1)} %param.35) | copy-start | bytes 8650756
  6.0 9.2 %copy-start.10 = (bf16[2048,64]{0,1:T(8,128)(2,1)S(1)}, bf16[2048,64]{0,1:T(8,128)(2,1)}, u32[]{:S(2)}) copy-start(bf16[2048,64]{0,1:T(8,128)(2,1)} %param.37) | copy-start | bytes 786436
  6.0 10.1 %copy-start.9 = (bf16[2048,64]{0,1:T(8,128)(2,1)S(1)}, bf16[2048,64]{0,1:T(8,128)(2,1)}, u32[]{:S(2)}) copy-start(bf16[2048,64]{0,1:T(8,128)(2,1)} %param.36) | copy-start | bytes 786436
  6.0 11.2 %copy-start.29 = (s32[32]{0:T(128)S(1)}, s32[32]{0:T(128)}, u32[]{:S(2)}) copy-start(s32[32]{0:T(128)} %param.25) | copy-start | bytes 388
  6.0 11.8 %copy-start.30 = (s32[32]{0:T(128)S(1)}, s32[32]{0:T(128)}, u32[]{:S(2)}) copy-start(s32[32]{0:T(128)} %param.24) | copy-start | bytes 388
  6.0 14.9 %copy-start.20 = (s32[256]{0:T(256)S(1)}, s32[256]{0:T(256)}, u32[]{:S(2)}) copy-start(s32[256]{0:T(256)} %param.21) | copy-start | bytes 3076
  6.0 14.9 %copy-start.26 = (s32[256]{0:T(256)S(1)}, s32[256]{0:T(256)}, u32[]{:S(2)}) copy-start(s32[256]{0:T(256)} %param.23) | copy-start | bytes 3076
  6.0 14.9 %copy-start.27 = (s32[256]{0:T(256)S(1)}, s32[256]{0:T(256)}, u32[]{:S(2)}) copy-start(s32[256]{0:T(256)} %param.22) | copy-start | bytes 3076
  6.0 192.7 %all-to-all-start = ((bf16[32,512,256]{2,1,0:T(8,128)(2,1)}), bf16[32,512,256]{2,1,0:T(8,128)(2,1)}, u32[]{:S(2)}, u32[]{:S(2)}) async-start(bf16[32,512,256]{2,1,0:T(8,128)(2,1)} %stack.34), calls=%async_computation | async-start | bytes 16777216 | tf_op jit(solution)/shard_map/all_to_all | solution.py:123
  15.2 195.4 %copy-start.16 = (f32[2048]{0:T(1024)S(1)}, f32[2048]{0:T(1024)}, u32[]{:S(2)}) copy-start(f32[2048]{0:T(1024)} %param.27) | copy-start | bytes 24580
  15.9 217.1 %collective-permute-start = (bf16[1792,64]{0,1:T(8,128)(2,1)}, bf16[1792,64]{0,1:T(8,128)(2,1)}, u32[]{:S(2)}, u32[]{:S(2)}) collective-permute-start(bf16[1792,64]{0,1:T(8,128)(2,1)} %slice.43), channel_id=1, source_target_pairs={{0,8},{8,0},{16,24},{24,16},{32,40},{40,32},{48,56},{56,48},{64,72... | collective-permute-start | bytes 688136 | tf_op jit(solution)/shard_map/ppermute | solution.py:17
  16.8 214.5 %collective-permute-start.5 = (bf16[1792,64]{0,1:T(8,128)(2,1)}, bf16[1792,64]{0,1:T(8,128)(2,1)}, u32[]{:S(2)}, u32[]{:S(2)}) collective-permute-start(bf16[1792,64]{0,1:T(8,128)(2,1)} %slice.45), channel_id=1, source_target_pairs={{0,8},{8,0},{16,24},{24,16},{32,40},{40,32},{48,56},{56,48},{64,72... | collective-permute-start | bytes 688136 | tf_op jit(solution)/shard_map/ppermute | solution.py:17
  21.0 192.5 %copy-start.21 = (pred[512]{0:T(512)(128)(4,1)}, pred[512]{0:T(512)(128)(4,1)S(1)}, u32[]{:S(2)}) copy-start(pred[512]{0:T(512)(128)(4,1)S(1)} %compare_and_fusion.1) | copy-start | bytes 1540
  204.7 20.2 %copy-start.4 = (bf16[512,256]{1,0:T(8,128)(2,1)}, bf16[512,256]{1,0:T(8,128)(2,1)S(1)}, u32[]{:S(2)}) copy-start(bf16[512,256]{1,0:T(8,128)(2,1)S(1)} %gather_fusion) | copy-start | bytes 786436
  205.6 18.1 %collective-permute-start.1 = (bf16[512,256]{1,0:T(8,128)(2,1)}, bf16[512,256]{1,0:T(8,128)(2,1)}, u32[]{:S(2)}, u32[]{:S(2)}) collective-permute-start(bf16[512,256]{1,0:T(8,128)(2,1)} %broadcast_select_fusion.2), channel_id=1, source_target_pairs={{0,1},{1,0},{2,3},{3,2},{4,5},{5,4},{6,7},{7,6},{8,9},{9,8},{10,11... | collective-permute-start | bytes 786440 | tf_op jit(solution)/shard_map/ppermute | solution.py:17
  213.5 19.6 %copy-start.11 = (bf16[2048,64]{0,1:T(8,128)(2,1)S(1)}, bf16[2048,64]{0,1:T(8,128)(2,1)}, u32[]{:S(2)}) copy-start(bf16[2048,64]{0,1:T(8,128)(2,1)} %param.37) | copy-start | bytes 786436
  224.9 16.5 %collective-permute-start.3 = (bf16[2,512,256]{2,1,0:T(8,128)(2,1)S(1)}, bf16[2,512,256]{2,1,0:T(8,128)(2,1)S(1)}, u32[]{:S(2)}, u32[]{:S(2)}) collective-permute-start(bf16[2,512,256]{2,1,0:T(8,128)(2,1)S(1)} %get-tuple-element.34), channel_id=1, source_target_pairs={{0,4},{1,5},{2,6},{3,7},{4,0},{5,1},{6,2},{7,3},{8,12},{9,13},{10,... | collective-permute-start | bytes 1572872 | tf_op jit(solution)/shard_map/ppermute | solution.py:13
  228.0 22.6 %collective-permute-start.2 = (bf16[2,512,256]{2,1,0:T(8,128)(2,1)S(1)}, bf16[2,512,256]{2,1,0:T(8,128)(2,1)S(1)}, u32[]{:S(2)}, u32[]{:S(2)}) collective-permute-start(bf16[2,512,256]{2,1,0:T(8,128)(2,1)S(1)} %get-tuple-element.34), channel_id=1, source_target_pairs={{0,2},{1,3},{2,4},{3,5},{4,6},{5,7},{6,0},{7,1},{8,10},{9,11},{10,... | collective-permute-start | bytes 1572872 | tf_op jit(solution)/shard_map/ppermute | solution.py:13
  228.6 22.1 %collective-permute-start.4 = (bf16[2,512,256]{2,1,0:T(8,128)(2,1)S(1)}, bf16[2,512,256]{2,1,0:T(8,128)(2,1)S(1)}, u32[]{:S(2)}, u32[]{:S(2)}) collective-permute-start(bf16[2,512,256]{2,1,0:T(8,128)(2,1)S(1)} %get-tuple-element.34), channel_id=1, source_target_pairs={{0,6},{1,7},{2,0},{3,1},{4,2},{5,3},{6,4},{7,5},{8,14},{9,15},{10,... | collective-permute-start | bytes 1572872 | tf_op jit(solution)/shard_map/ppermute | solution.py:13
  252.4 3.7 copy-start.18
  256.1 2.4 copy-start.1
  266.6 8.0 %copy-start.17 = (f32[4,2,256]{2,1,0:T(2,128)S(1)}, f32[4,2,256]{2,1,0:T(2,128)}, u32[]{:S(2)}) copy-start(f32[4,2,256]{2,1,0:T(2,128)} %mul.193) | copy-start | bytes 24580
  282.4 2.7 copy-start.12
  285.1 0.7 copy-start.25
  293.1 2.7 copy-start.14
  293.1 2.7 copy-start.15
  293.1 2.8 copy-start.7
  308.5 15.6 %copy-start.3 = (f32[2,256,2048]{2,1,0:T(8,128)S(1)}, f32[2,256,2048]{2,1,0:T(8,128)}, u32[]{:S(2)}) copy-start(f32[2,256,2048]{2,1,0:T(8,128)} %reshape.516) | copy-start | bytes 12582916
  308.5 15.6 %copy-start.13 = (bf16[2048,64]{0,1:T(8,128)(2,1)S(1)}, bf16[2048,64]{0,1:T(8,128)(2,1)}, u32[]{:S(2)}) copy-start(bf16[2048,64]{0,1:T(8,128)(2,1)} %param.30) | copy-start | bytes 786436
  308.5 15.6 %copy-start.24 = (f32[2,256]{1,0:T(2,128)S(1)}, f32[2,256]{1,0:T(2,128)}, u32[]{:S(2)}) copy-start(f32[2,256]{1,0:T(2,128)} %rsqrt.21) | copy-start | bytes 6148
  325.1 16.0 %copy-start.8 = (bf16[256,2048]{1,0:T(8,128)(2,1)S(1)}, bf16[256,2048]{1,0:T(8,128)(2,1)}, u32[]{:S(2)}) copy-start(bf16[256,2048]{1,0:T(8,128)(2,1)} %param.31) | copy-start | bytes 3145732
  356.7 25.3 %collective-permute-start.8 = (bf16[512,512]{1,0:T(8,128)(2,1)S(1)}, bf16[512,512]{1,0:T(8,128)(2,1)}, u32[]{:S(2)}, u32[]{:S(2)}) collective-permute-start(bf16[512,512]{1,0:T(8,128)(2,1)S(1)} %fusion.47), channel_id=1, source_target_pairs={{0,6},{1,7},{2,0},{3,1},{4,2},{5,3},{6,4},{7,5},{8,14},{9,15},{10,... | collective-permute-start | bytes 1572872 | tf_op jit(solution)/shard_map/ppermute | solution.py:13
  360.3 26.3 %collective-permute-start.6 = (bf16[512,512]{1,0:T(8,128)(2,1)}, bf16[512,512]{1,0:T(8,128)(2,1)}, u32[]{:S(2)}, u32[]{:S(2)}) collective-permute-start(bf16[512,512]{1,0:T(8,128)(2,1)} %fusion.49), channel_id=1, source_target_pairs={{0,2},{1,3},{2,4},{3,5},{4,6},{5,7},{6,0},{7,1},{8,10},{9,11},{10,... | collective-permute-start | bytes 1572872 | tf_op jit(solution)/shard_map/ppermute | solution.py:13
  361.2 25.4 %collective-permute-start.7 = (bf16[512,512]{1,0:T(8,128)(2,1)}, bf16[512,512]{1,0:T(8,128)(2,1)}, u32[]{:S(2)}, u32[]{:S(2)}) collective-permute-start(bf16[512,512]{1,0:T(8,128)(2,1)} %fusion.48), channel_id=1, source_target_pairs={{0,4},{1,5},{2,6},{3,7},{4,0},{5,1},{6,2},{7,3},{8,12},{9,13},{10,... | collective-permute-start | bytes 1572872 | tf_op jit(solution)/shard_map/ppermute | solution.py:13
  394.4 19.0 %copy-start.22 = (pred[512]{0:T(512)(128)(4,1)S(1)}, pred[512]{0:T(512)(128)(4,1)}, u32[]{:S(2)}) copy-start(pred[512]{0:T(512)(128)(4,1)} %copy-done.21) | copy-start | bytes 1540
  398.8 14.6 %collective-permute-start.9 = (bf16[512,256]{1,0:T(8,128)(2,1)S(1)}, bf16[512,256]{1,0:T(8,128)(2,1)S(1)}, u32[]{:S(2)}, u32[]{:S(2)}) collective-permute-start(bf16[512,256]{1,0:T(8,128)(2,1)S(1)} %fusion.55), channel_id=1, source_target_pairs={{0,1},{1,0},{2,3},{3,2},{4,5},{5,4},{6,7},{7,6},{8,9},{9,8},{10,11... | collective-permute-start | bytes 786440 | tf_op jit(solution)/shard_map/ppermute | solution.py:17
  414.5 12.1 %copy-start.5 = (bf16[512,256]{1,0:T(8,128)(2,1)}, bf16[512,256]{1,0:T(8,128)(2,1)S(1)}, u32[]{:S(2)}) copy-start(bf16[512,256]{1,0:T(8,128)(2,1)S(1)} %fusion.54) | copy-start | bytes 786436
  414.6 12.1 %collective-permute-start.10 = (bf16[512,256]{1,0:T(8,128)(2,1)S(1)}, bf16[512,256]{1,0:T(8,128)(2,1)S(1)}, u32[]{:S(2)}, u32[]{:S(2)}) collective-permute-start(bf16[512,256]{1,0:T(8,128)(2,1)S(1)} %fusion.54), channel_id=1, source_target_pairs={{0,1},{1,0},{2,3},{3,2},{4,5},{5,4},{6,7},{7,6},{8,9},{9,8},{10,11... | collective-permute-start | bytes 786440 | tf_op jit(solution)/shard_map/ppermute | solution.py:17
  426.8 16.5 %collective-permute-start.12 = (bf16[2,512,256]{2,1,0:T(8,128)(2,1)S(1)}, bf16[2,512,256]{2,1,0:T(8,128)(2,1)S(1)}, u32[]{:S(2)}, u32[]{:S(2)}) collective-permute-start(bf16[2,512,256]{2,1,0:T(8,128)(2,1)S(1)} %get-tuple-element.30), channel_id=1, source_target_pairs={{0,4},{1,5},{2,6},{3,7},{4,0},{5,1},{6,2},{7,3},{8,12},{9,13},{10,... | collective-permute-start | bytes 1572872 | tf_op jit(solution)/shard_map/ppermute | solution.py:13
  427.8 24.7 %collective-permute-start.11 = (bf16[2,512,256]{2,1,0:T(8,128)(2,1)S(1)}, bf16[2,512,256]{2,1,0:T(8,128)(2,1)S(1)}, u32[]{:S(2)}, u32[]{:S(2)}) collective-permute-start(bf16[2,512,256]{2,1,0:T(8,128)(2,1)S(1)} %get-tuple-element.30), channel_id=1, source_target_pairs={{0,2},{1,3},{2,4},{3,5},{4,6},{5,7},{6,0},{7,1},{8,10},{9,11},{10,... | collective-permute-start | bytes 1572872 | tf_op jit(solution)/shard_map/ppermute | solution.py:13
  427.8 24.7 %collective-permute-start.13 = (bf16[2,512,256]{2,1,0:T(8,128)(2,1)S(1)}, bf16[2,512,256]{2,1,0:T(8,128)(2,1)S(1)}, u32[]{:S(2)}, u32[]{:S(2)}) collective-permute-start(bf16[2,512,256]{2,1,0:T(8,128)(2,1)S(1)} %get-tuple-element.30), channel_id=1, source_target_pairs={{0,6},{1,7},{2,0},{3,1},{4,2},{5,3},{6,4},{7,5},{8,14},{9,15},{10,... | collective-permute-start | bytes 1572872 | tf_op jit(solution)/shard_map/ppermute | solution.py:13
  454.2 3.7 copy-start.19
  457.9 2.4 copy-start.2
  462.7 5.3 copy-start.23
  468.0 4.1 copy-start.28
  470.8 1.4 copy-start.6
  495.5 14.9 %collective-permute-start.16 = (bf16[512,512]{1,0:T(8,128)(2,1)S(1)}, bf16[512,512]{1,0:T(8,128)(2,1)S(1)}, u32[]{:S(2)}, u32[]{:S(2)}) collective-permute-start(bf16[512,512]{1,0:T(8,128)(2,1)S(1)} %fusion.43), channel_id=1, source_target_pairs={{0,6},{1,7},{2,0},{3,1},{4,2},{5,3},{6,4},{7,5},{8,14},{9,15},{10,... | collective-permute-start | bytes 1572872 | tf_op jit(solution)/shard_map/ppermute | solution.py:13
  496.2 25.8 %collective-permute-start.14 = (bf16[512,512]{1,0:T(8,128)(2,1)S(1)}, bf16[512,512]{1,0:T(8,128)(2,1)S(1)}, u32[]{:S(2)}, u32[]{:S(2)}) collective-permute-start(bf16[512,512]{1,0:T(8,128)(2,1)S(1)} %fusion.45), channel_id=1, source_target_pairs={{0,2},{1,3},{2,4},{3,5},{4,6},{5,7},{6,0},{7,1},{8,10},{9,11},{10,... | collective-permute-start | bytes 1572872 | tf_op jit(solution)/shard_map/ppermute | solution.py:13
  497.6 24.4 %collective-permute-start.15 = (bf16[512,512]{1,0:T(8,128)(2,1)S(1)}, bf16[512,512]{1,0:T(8,128)(2,1)S(1)}, u32[]{:S(2)}, u32[]{:S(2)}) collective-permute-start(bf16[512,512]{1,0:T(8,128)(2,1)S(1)} %fusion.44), channel_id=1, source_target_pairs={{0,4},{1,5},{2,6},{3,7},{4,0},{5,1},{6,2},{7,3},{8,12},{9,13},{10,... | collective-permute-start | bytes 1572872 | tf_op jit(solution)/shard_map/ppermute | solution.py:13
  532.4 10.4 %collective-permute-start.17 = (bf16[512,256]{1,0:T(8,128)(2,1)S(1)}, bf16[512,256]{1,0:T(8,128)(2,1)S(1)}, u32[]{:S(2)}, u32[]{:S(2)}) collective-permute-start(bf16[512,256]{1,0:T(8,128)(2,1)S(1)} %fusion.56), channel_id=1, source_target_pairs={{0,1},{1,0},{2,3},{3,2},{4,5},{5,4},{6,7},{7,6},{8,9},{9,8},{10,11... | collective-permute-start | bytes 786440 | tf_op jit(solution)/shard_map/ppermute | solution.py:17
